TPU v7x, 512 devices: a whole 4x4x16 slice. The times are simulated.
512 devices in a mesh: rep: 8 (over y, core), expert: 64 (over x, z).
Axes of the slice: x: 4, y: 4, z: 16, core: 2. Of those that a mesh axis runs over, the one named last changes fastest.
Arguments:
- tokens: bfloat16 [8192, 4096], P('expert', 'rep')
- norm_gain: float32 [4096], P('rep'), may hold values from 0.25 to 1.75
- gate_weights: float32 [8192, 8], P('expert'), may hold values from 0.1 to 0.6
- exit_flags: int32 [8192], P('expert'), may hold values from 0 to 1, as said below
- routes: int32 [8192, 8], P('expert'), may hold values from 0 to 127, as said below
- next_device: int32 [8192], P('expert'), may hold values from 0 to 63, as said below
- up_weight: bfloat16 [128, 4096, 1024], P('expert', 'rep'), may hold values from -0.09375 to 0.09375
- down_weight: bfloat16 [128, 1024, 4096], P('expert', None, 'rep'), may hold values from -0.1875 to 0.1875
Outputs:
- handed: float32 [4096, 4096], P('expert', 'rep')
Inputs may be any that keep to these rules, and one draw needn't show every extreme that they name: `exit_flags`: one block of 128 rows holds at most 64 live rows; some block holds exactly 64. `routes`: each row names 8 different experts. Among the live rows of one block, every expert is named the same number of times up to one, so at most 4 times; a block with 64 live rows names every expert exactly 4 times. `next_device`: among the live rows of one block, every value is named the same number of times up to one, so at most 1 times.
All inputs are finite; a program needn't handle non-finite values.
Results may differ from a plain program's by a relative error of at most 0.0017.
Values may be sent and summed in bfloat16 or wider, within the bound.
No kernel may reach another device: no remote copies, remote signals or barrier semaphores. Data moves between devices by JAX's collectives and lax.ppermute only.
A program may use at most 64 MiB of HBM per device.

v0:
```python
import jax
import jax.numpy as jnp
from jax import lax
from jax.sharding import PartitionSpec as P


def per_device(
    tokens, norm_gain, gate_weights, exit_flags, routes, next_device, up_weight, down_weight
):
    row_count, feat_width = tokens.shape
    owner_count = lax.axis_size("expert")
    rep_count = lax.axis_size("rep")
    local_experts = up_weight.shape[0]
    route_count = routes.shape[1]
    experts_all = local_experts * owner_count
    most_live = row_count // 2
    capacity = route_count * most_live // experts_all
    hand_cap = (most_live + owner_count - 1) // owner_count
    slot_total = local_experts * owner_count * capacity
    widened = tokens.astype(jnp.float32)
    squares = lax.psum(jnp.sum(widened * widened, axis=1), "rep")
    rinv_rows = lax.rsqrt(squares / (feat_width * rep_count) + 1e-06)
    normed = (widened * rinv_rows[:, None] * norm_gain[None, :]).astype(jnp.bfloat16)
    survive = 1 - exit_flags
    pair_live = jnp.repeat(survive, route_count)
    route_flat = routes.reshape(-1)
    one_hot = (route_flat[:, None] == jnp.arange(experts_all, dtype=jnp.int32)[None, :]).astype(
        jnp.int32
    ) * pair_live[:, None]
    earlier = jnp.cumsum(one_hot, axis=0) - one_hot
    position = jnp.sum(earlier * one_hot, axis=1)
    owner_id = route_flat // local_experts
    local_id = route_flat % local_experts
    slot_index = (local_id * owner_count + owner_id) * capacity + position
    slot_index = jnp.where(pair_live > 0, slot_index, slot_total)
    pair_row = jnp.arange(row_count * route_count, dtype=jnp.int32) // route_count
    source_row = jnp.zeros((slot_total,), jnp.int32).at[slot_index].set(pair_row + 1, mode="drop")
    padded = jnp.concatenate([jnp.zeros((1, feat_width), jnp.bfloat16), normed], axis=0)
    outbound = padded[source_row].reshape(local_experts, owner_count, capacity, feat_width)
    received = lax.all_to_all(outbound, "expert", split_axis=1, concat_axis=1, tiled=True)
    item_count = received.shape[2]
    flattened = received.reshape(local_experts, owner_count * item_count, feat_width)
    partial_value = jnp.einsum(
        "erd,edh->erh", flattened, up_weight, preferred_element_type=jnp.float32
    )
    summed = lax.psum(partial_value, "rep")
    activated = jax.nn.silu(summed).astype(jnp.bfloat16)
    expert_out = jnp.einsum(
        "erh,ehd->erd", activated, down_weight, preferred_element_type=jnp.float32
    )
    expert_out = expert_out.astype(jnp.bfloat16).reshape(
        local_experts, owner_count, item_count, feat_width
    )
    returned = lax.all_to_all(expert_out, "expert", split_axis=1, concat_axis=1, tiled=True)
    flat_back = returned.reshape(slot_total, feat_width)
    picked = flat_back[jnp.minimum(slot_index, slot_total - 1)].reshape(
        row_count, route_count, feat_width
    )
    mixture = jnp.einsum("rk,rkd->rd", gate_weights, picked, preferred_element_type=jnp.float32)
    updated = widened + mixture
    dest_hot = (next_device[:, None] == jnp.arange(owner_count, dtype=jnp.int32)[None, :]).astype(
        jnp.int32
    ) * survive[:, None]
    dest_before = jnp.cumsum(dest_hot, axis=0) - dest_hot
    handoff_pos = jnp.sum(dest_before * dest_hot, axis=1)
    hand_slot = jnp.where(survive > 0, next_device * hand_cap + handoff_pos, owner_count * hand_cap)
    row_plus = jnp.arange(row_count, dtype=jnp.int32) + 1
    target = (
        jnp.zeros((owner_count * hand_cap,), jnp.int32).at[hand_slot].set(row_plus, mode="drop")
    )
    stacked = jnp.concatenate([jnp.zeros((1, feat_width), jnp.float32), updated], axis=0)
    leaving = stacked[target].reshape(owner_count, hand_cap, feat_width)
    arrived = lax.all_to_all(leaving, "expert", split_axis=0, concat_axis=0, tiled=True)
    return arrived.reshape(owner_count * hand_cap, feat_width)


def solution(mesh):
    in_specs = (
        P("expert", "rep"),
        P("rep"),
        P("expert", None),
        P("expert"),
        P("expert", None),
        P("expert"),
        P("expert", "rep", None),
        P("expert", None, "rep"),
    )
    out_specs = P("expert", "rep")
    return jax.shard_map(
        per_device, mesh=mesh, in_specs=in_specs, out_specs=out_specs, check_vma=False
    )
```

profile of v0, /device:TPU:24, one launch (start us, length us, event | category | flops | bytes accessed | tf_op | source)
XLA Modules:
  0.0 243.5 jit_solution(2612807899074196465)
XLA Ops:
  6.5 0.9 copy.16
  7.8 0.7 broadcast_subtract_fusion
  8.4 0.7 broadcast_compare_fusion
  9.4 0.3 fusion.3
  10.3 0.5 fusion.2
  10.8 4.3 %scatter_custom_fusion = s32[512]{0:T(512)S(1)} fusion(s32[1024]{0:T(1024)S(1)} %bitcast.29, s32[1024]{0:T(1024)S(1)} %fusion.13, s32[]{:T(128)} %constant.69.clone.1), kind=kCustom, calls=%fused_computation.56 | custom fusion | bytes 2052 | tf_op jit(solution)/shard_map/scatter | solution.py:37
  15.3 14.0 %psum.14 = f32[128]{0:T(128)S(1)} all-reduce(f32[128]{0:T(128)S(1)} %fusion.5), channel_id=1, replica_groups=mesh['rep'=8,'expert'=64] {'rep'}, use_global_device_ids=true, to_apply=%region_1.0 | all-reduce | flops 128 | bytes 1024 | tf_op jit(solution)/shard_map/psum | solution.py:21
  29.5 2.0 gather_fusion
  31.6 0.2 copy.22
  31.8 46.3 %all_to_all.15 = bf16[2,64,4,512]{3,2,0,1:T(4,128)(2,1)S(1)} all-to-all(bf16[2,64,4,512]{3,2,0,1:T(4,128)(2,1)S(1)} %copy.22), channel_id=1, replica_groups=mesh['rep'=8,'expert'=64] {'expert'}, dimensions={1} | all-to-all | bytes 1048576 | tf_op jit(solution)/shard_map/all_to_all | solution.py:40
  78.1 0.2 copy.23
  78.4 2.0 fusion.25
  80.5 72.3 %all-reduce.4.cloned.1.call-done = f32[2,256,1024]{2,1,0:T(8,128)} async-done(((f32[2,256,1024]{2,1,0:T(8,128)}), f32[2,256,1024]{2,1,0:T(8,128)}) %all-reduce.4.cloned.1.call-update) | async-done | bytes 2097168 | tf_op jit(solution)/shard_map/psum | solution.py:46
  152.8 3.0 %convolution_convert_fusion = bf16[2,256,512]{2,1,0:T(8,128)(2,1)S(1)} fusion(bf16[2,1024,512]{2,1,0:T(8,128)(2,1)} %param.15, f32[2,256,1024]{2,1,0:T(8,128)} %all-reduce.4.cloned.1.call-done), kind=kOutput, calls=%fused_computation.6 | convolution fusion | flops 539754496 | bytes 4718592 | tf_op jit(solution)/shard_map/erh,ehd->erd/dot_general | solution.py:48
  155.9 1.0 copy.24
  156.9 15.6 %all-to-all-start.1 = ((bf16[2,64,4,512]{3,2,0,1:T(4,128)(2,1)}), bf16[2,64,4,512]{3,2,0,1:T(4,128)(2,1)S(1)}, u32[]{:S(2)}, u32[]{:S(2)}) async-start(bf16[2,64,4,512]{3,2,0,1:T(4,128)(2,1)} %copy.24), calls=%async_computation.1 | async-start | bytes 1048576 | tf_op jit(solution)/shard_map/all_to_all | solution.py:54
  173.2 1.0 scatter_custom_fusion.1
  174.2 29.5 %all-to-all-done.1 = bf16[2,64,4,512]{3,2,0,1:T(4,128)(2,1)S(1)} async-done(((bf16[2,64,4,512]{3,2,0,1:T(4,128)(2,1)}), bf16[2,64,4,512]{3,2,0,1:T(4,128)(2,1)S(1)}, u32[]{:S(2)}, u32[]{:S(2)}) %all-to-all-start.1) | async-done | bytes 524320 | tf_op jit(solution)/shard_map/all_to_all | solution.py:54
  203.7 0.2 copy.25
  204.0 5.1 %gather_fusion.1 = bf16[1024,512]{1,0:T(8,128)(2,1)} fusion(bf16[512,512]{1,0:T(8,128)(2,1)S(1)} %reshape.231, s32[1024]{0:T(1024)S(1)} %broadcast_clamp_fusion), kind=kCustom, calls=%fused_computation.1 | custom fusion | bytes 2101248 | tf_op jit(solution)/shard_map/gather | solution.py:56
  209.0 1.6 fusion
  210.8 0.7 gather_fusion.2
  211.6 24.5 %all_to_all.16 = f32[64,1,512]{2,1,0:T(1,128)S(1)} all-to-all(f32[64,1,512]{2,1,0:T(1,128)S(1)} %copy.26), channel_id=1, replica_groups=mesh['rep'=8,'expert'=64] {'expert'}, dimensions={0} | all-to-all | bytes 262144 | tf_op jit(solution)/shard_map/all_to_all | solution.py:73
  236.0 0.7 copy.32
  (54 shorter events, 2.7 us)
Async XLA Ops:
  6.5 71.9 %copy-start = (bf16[2,512,1024]{2,1,0:T(8,128)(2,1)S(1)}, bf16[2,512,1024]{2,1,0:T(8,128)(2,1)}, u32[]{:S(2)}) copy-start(bf16[2,512,1024]{2,1,0:T(8,128)(2,1)} %param.14) | copy-start | bytes 6291460
  6.5 8.6 %copy-start.1 = (bf16[128,512]{1,0:T(8,128)(2,1)S(1)}, bf16[128,512]{1,0:T(8,128)(2,1)}, u32[]{:S(2)}) copy-start(bf16[128,512]{1,0:T(8,128)(2,1)} %param.8) | copy-start | bytes 393220
  6.5 22.8 %copy-start.4 = (f32[512]{0:T(512)S(1)}, f32[512]{0:T(512)}, u32[]{:S(2)}) copy-start(f32[512]{0:T(512)} %param.9) | copy-start | bytes 6148
  6.5 146.2 %all-reduce.4.cloned.1.call-start = ((), (), s32[]{:S(2)}) async-start(), calls=%async_computation.3 | async-start | bytes 4194304 | tf_op jit(solution)/shard_map/psum | solution.py:46
  155.8 16.8 %copy-start.3 = (f32[128,8]{0,1:T(8,128)S(1)}, f32[128,8]{0,1:T(8,128)}, u32[]{:S(2)}) copy-start(f32[128,8]{0,1:T(8,128)} %param.10) | copy-start | bytes 12292
  155.8 16.9 %copy-start.2 = (s32[128]{0:T(128)S(1)}, s32[128]{0:T(128)}, u32[]{:S(2)}) copy-start(s32[128]{0:T(128)} %param.13) | copy-start | bytes 1540
  155.8 17.4 %copy-start.5 = (s32[128]{0:T(128)S(1)}, s32[128]{0:T(128)}, u32[]{:S(2)}) copy-start(s32[128]{0:T(128)} %param.11) | copy-start | bytes 1540
  156.9 46.8 %all-to-all-start.1 = ((bf16[2,64,4,512]{3,2,0,1:T(4,128)(2,1)}), bf16[2,64,4,512]{3,2,0,1:T(4,128)(2,1)S(1)}, u32[]{:S(2)}, u32[]{:S(2)}) async-start(bf16[2,64,4,512]{3,2,0,1:T(4,128)(2,1)} %copy.24), calls=%async_computation.1 | async-start | bytes 1048576 | tf_op jit(solution)/shard_map/all_to_all | solution.py:54
Sparse Core Ops, SparseCore 0:
  80.6 72.1 all-reduce.3
where the time goes:
time: 244 us
  waiting for transfers between devices  102 us (42%)
  blocking collectives  84.8 us (35%)
  local copies, waits for them, and re-layouts  18 us (7%)
  starting transfers between devices  15.6 us (6%)
  between operations  13.7 us (6%)
  matrix products  6.6 us (3%)
  other arithmetic  3.01 us (1%)
    psum x1, waiting for transfers between devices, per_device(): summed = lax.psum(partial_value, 'rep')  72.3 us
    all_to_all x1, blocking collectives, per_device(): lax.all_to_all(outbound, 'expert', split_axis=1, concat_axis=1, tiled=True)  46.3 us
    all_to_all x1, waiting for transfers between devices, per_device(): lax.all_to_all(expert_out, 'expert', split_axis=1, concat_axis=1, tiled=T...  29.5 us
    all_to_all x1, blocking collectives, per_device(): lax.all_to_all(leaving, 'expert', split_axis=0, concat_axis=0, tiled=True)  24.5 us
    all_to_all x1, starting transfers between devices, per_device(): lax.all_to_all(expert_out, 'expert', split_axis=1, concat_axis=1, tiled=T...  15.6 us
    psum x1, blocking collectives, per_device(): squares = lax.psum(jnp.sum(widened * widened, axis=1), 'rep')  14 us
    gather x1, local copies, waits for them, and re-layouts, per_device(): flat_back[jnp.minimum(slot_index, slot_total - 1)]  5.07 us
  transfers between devices with their start and end apart: 2, of which 2 were waited for; matrix products, arithmetic and copies ran while one was open for 1% of the time, Pallas kernels for 0%

commit v1 on v0

--- a/solution.py
+++ b/solution.py
@@ -43,7 +43,9 @@
     partial_value = jnp.einsum(
         "erd,edh->erh", flattened, up_weight, preferred_element_type=jnp.float32
     )
-    summed = lax.psum(partial_value, "rep")
+    summed = partial_value
+    for hop in (1, 2, 4):
+        summed = summed + lax.ppermute(summed, "rep", [(dev, dev ^ hop) for dev in range(8)])
     activated = jax.nn.silu(summed).astype(jnp.bfloat16)
     expert_out = jnp.einsum(
         "erh,ehd->erd", activated, down_weight, preferred_element_type=jnp.float32

time: 244 us -> 252 us (1.033)
  waiting for transfers between devices: 102 us -> 127 us
  between operations: 13.7 us -> 0.39 us
  matrix products: 6.6 us -> 3.08 us
    ppermute x0 -> x3, waiting for transfers between devices: none -> 99.3 us  [per_device(): lax.ppermute(summed, 'rep', [(dev, dev ^ hop) for dev in range(8)])]
    psum x1 -> x0, waiting for transfers between devices: 72.3 us -> none  [per_device(): summed = lax.psum(partial_value, 'rep')]
    all_to_all x1, starting transfers between devices: 15.6 us -> 6.74 us  [per_device(): lax.all_to_all(expert_out, 'expert', split_axis=1, concat_axis=1, tiled=T...]
    ppermute x0 -> x3, starting transfers between devices: none -> 7.95 us  [per_device(): lax.ppermute(summed, 'rep', [(dev, dev ^ hop) for dev in range(8)])]
  transfers between devices with their start and end apart: 2 -> 4, of which waited for: 2 -> 4; matrix products, arithmetic and copies ran while one was open for 1% -> 1% of each run, Pallas kernels for 0% -> 0%
where the time goes in v1:
time: 252 us; the launch traced here: 251 us
  waiting for transfers between devices  127 us (50%)
  blocking collectives  82.9 us (33%)
  local copies, waits for them, and re-layouts  18 us (7%)
  starting transfers between devices  14.7 us (6%)
  other arithmetic  4.11 us (2%)
  matrix products  3.08 us (1%)
    ppermute x3, waiting for transfers between devices, per_device(): lax.ppermute(summed, 'rep', [(dev, dev ^ hop) for dev in range(8)])  99.3 us
    all_to_all x1, blocking collectives, per_device(): lax.all_to_all(outbound, 'expert', split_axis=1, concat_axis=1, tiled=True)  46.3 us
    all_to_all x1, waiting for transfers between devices, per_device(): lax.all_to_all(expert_out, 'expert', split_axis=1, concat_axis=1, tiled=T...  28.2 us
    all_to_all x1, blocking collectives, per_device(): lax.all_to_all(leaving, 'expert', split_axis=0, concat_axis=0, tiled=True)  22.5 us
    psum x1, blocking collectives, per_device(): squares = lax.psum(jnp.sum(widened * widened, axis=1), 'rep')  14 us
    ppermute x3, starting transfers between devices, per_device(): lax.ppermute(summed, 'rep', [(dev, dev ^ hop) for dev in range(8)])  7.95 us
    all_to_all x1, starting transfers between devices, per_device(): lax.all_to_all(expert_out, 'expert', split_axis=1, concat_axis=1, tiled=T...  6.74 us
    gather x1, local copies, waits for them, and re-layouts, per_device(): flat_back[jnp.minimum(slot_index, slot_total - 1)]  5.07 us
  transfers between devices with their start and end apart: 4, of which 4 were waited for; matrix products, arithmetic and copies ran while one was open for 1% of the time, Pallas kernels for 0%

profile of v1, /device:TPU:24, one launch (start us, length us, event | category | flops | bytes accessed | tf_op | source)
XLA Modules:
  0.0 250.6 jit_solution(6085079943754631807)
XLA Ops:
  0.0 0.9 copy.16
  1.2 0.7 broadcast_subtract_fusion
  1.9 0.7 broadcast_compare_fusion
  4.3 4.3 %scatter_custom_fusion = s32[512]{0:T(512)S(1)} fusion(s32[1024]{0:T(1024)S(1)} %bitcast.29, s32[1024]{0:T(1024)S(1)} %fusion.13, s32[]{:T(128)} %constant.69.clone.1), kind=kCustom, calls=%fused_computation.56 | custom fusion | bytes 2052 | tf_op jit(solution)/shard_map/scatter | solution.py:37
  8.8 14.0 %psum.7 = f32[128]{0:T(128)S(1)} all-reduce(f32[128]{0:T(128)S(1)} %fusion.5), channel_id=1, replica_groups=mesh['rep'=8,'expert'=64] {'rep'}, use_global_device_ids=true, to_apply=%region_1.0 | all-reduce | flops 128 | bytes 1024 | tf_op jit(solution)/shard_map/psum | solution.py:21
  23.0 2.0 gather_fusion
  25.3 46.3 %all_to_all.15 = bf16[2,64,4,512]{3,2,0,1:T(4,128)(2,1)S(1)} all-to-all(bf16[2,64,4,512]{3,2,0,1:T(4,128)(2,1)S(1)} %copy.22), channel_id=1, replica_groups=mesh['rep'=8,'expert'=64] {'expert'}, dimensions={1} | all-to-all | bytes 1048576 | tf_op jit(solution)/shard_map/all_to_all | solution.py:40
  71.9 0.7 fusion.25
  72.6 3.1 %collective-permute-start = (f32[2,256,1024]{2,1,0:T(8,128)S(1)}, f32[2,256,1024]{2,1,0:T(8,128)S(1)}, u32[]{:S(2)}, u32[]{:S(2)}) collective-permute-start(f32[2,256,1024]{2,1,0:T(8,128)S(1)} %fusion.25), channel_id=1, source_target_pairs={{0,64},{64,0},{128,192},{192,128},{256,320},{320,256},{384,448},{4... | collective-permute-start | bytes 6291464 | tf_op jit(solution)/shard_map/ppermute | solution.py:48
  75.7 3.8 %collective-permute-done = f32[2,256,1024]{2,1,0:T(8,128)S(1)} collective-permute-done((f32[2,256,1024]{2,1,0:T(8,128)S(1)}, f32[2,256,1024]{2,1,0:T(8,128)S(1)}, u32[]{:S(2)}, u32[]{:S(2)}) %collective-permute-start) | collective-permute-done | bytes 2097184 | tf_op jit(solution)/shard_map/ppermute | solution.py:48
  80.1 2.1 collective-permute-start.1
  82.1 47.9 %collective-permute-done.1 = f32[2,256,1024]{2,1,0:T(8,128)S(1)} collective-permute-done((f32[2,256,1024]{2,1,0:T(8,128)S(1)}, f32[2,256,1024]{2,1,0:T(8,128)S(1)}, u32[]{:S(2)}, u32[]{:S(2)}) %collective-permute-start.1) | collective-permute-done | bytes 2097184 | tf_op jit(solution)/shard_map/ppermute | solution.py:48
  130.6 2.8 %collective-permute-start.2 = (f32[2,256,1024]{2,1,0:T(8,128)S(1)}, f32[2,256,1024]{2,1,0:T(8,128)S(1)}, u32[]{:S(2)}, u32[]{:S(2)}) collective-permute-start(f32[2,256,1024]{2,1,0:T(8,128)S(1)} %add.142), channel_id=1, source_target_pairs={{0,256},{64,320},{128,384},{192,448},{256,0},{320,64},{384,128},{4... | collective-permute-start | bytes 6291464 | tf_op jit(solution)/shard_map/ppermute | solution.py:48
  133.4 47.7 %collective-permute-done.2 = f32[2,256,1024]{2,1,0:T(8,128)S(1)} collective-permute-done((f32[2,256,1024]{2,1,0:T(8,128)S(1)}, f32[2,256,1024]{2,1,0:T(8,128)S(1)}, u32[]{:S(2)}, u32[]{:S(2)}) %collective-permute-start.2) | collective-permute-done | bytes 2097184 | tf_op jit(solution)/shard_map/ppermute | solution.py:48
  181.0 0.7 convolution_convert_fusion
  181.9 1.0 copy.24
  182.9 6.7 %all-to-all-start.1 = ((bf16[2,64,4,512]{3,2,0,1:T(4,128)(2,1)}), bf16[2,64,4,512]{3,2,0,1:T(4,128)(2,1)S(1)}, u32[]{:S(2)}, u32[]{:S(2)}) async-start(bf16[2,64,4,512]{3,2,0,1:T(4,128)(2,1)} %copy.24), calls=%async_computation.1 | async-start | bytes 1048576 | tf_op jit(solution)/shard_map/all_to_all | solution.py:56
  190.3 1.0 scatter_custom_fusion.1
  191.3 28.2 %all-to-all-done.1 = bf16[2,64,4,512]{3,2,0,1:T(4,128)(2,1)S(1)} async-done(((bf16[2,64,4,512]{3,2,0,1:T(4,128)(2,1)}), bf16[2,64,4,512]{3,2,0,1:T(4,128)(2,1)S(1)}, u32[]{:S(2)}, u32[]{:S(2)}) %all-to-all-start.1) | async-done | bytes 524320 | tf_op jit(solution)/shard_map/all_to_all | solution.py:56
  219.8 5.1 %gather_fusion.1 = bf16[1024,512]{1,0:T(8,128)(2,1)} fusion(bf16[512,512]{1,0:T(8,128)(2,1)S(1)} %reshape.231, s32[1024]{0:T(1024)S(1)} %broadcast_clamp_fusion), kind=kCustom, calls=%fused_computation.1 | custom fusion | bytes 2101248 | tf_op jit(solution)/shard_map/gather | solution.py:58
  224.9 1.6 fusion
  226.6 0.7 gather_fusion.2
  227.4 22.5 %all_to_all.16 = f32[64,1,512]{2,1,0:T(1,128)S(1)} all-to-all(f32[64,1,512]{2,1,0:T(1,128)S(1)} %copy.26), channel_id=1, replica_groups=mesh['rep'=8,'expert'=64] {'expert'}, dimensions={0} | all-to-all | bytes 262144 | tf_op jit(solution)/shard_map/all_to_all | solution.py:75
  249.9 0.7 copy.32
  (61 shorter events, 5.2 us)
Async XLA Ops:
  0.0 71.9 %copy-start = (bf16[2,512,1024]{2,1,0:T(8,128)(2,1)S(1)}, bf16[2,512,1024]{2,1,0:T(8,128)(2,1)}, u32[]{:S(2)}) copy-start(bf16[2,512,1024]{2,1,0:T(8,128)(2,1)} %param.14) | copy-start | bytes 6291460
  0.0 8.6 %copy-start.1 = (bf16[128,512]{1,0:T(8,128)(2,1)S(1)}, bf16[128,512]{1,0:T(8,128)(2,1)}, u32[]{:S(2)}) copy-start(bf16[128,512]{1,0:T(8,128)(2,1)} %param.8) | copy-start | bytes 393220
  0.0 22.8 %copy-start.4 = (f32[512]{0:T(512)S(1)}, f32[512]{0:T(512)}, u32[]{:S(2)}) copy-start(f32[512]{0:T(512)} %param.9) | copy-start | bytes 6148
  72.6 6.9 %collective-permute-start = (f32[2,256,1024]{2,1,0:T(8,128)S(1)}, f32[2,256,1024]{2,1,0:T(8,128)S(1)}, u32[]{:S(2)}, u32[]{:S(2)}) collective-permute-start(f32[2,256,1024]{2,1,0:T(8,128)S(1)} %fusion.25), channel_id=1, source_target_pairs={{0,64},{64,0},{128,192},{192,128},{256,320},{320,256},{384,448},{4... | collective-permute-start | bytes 6291464 | tf_op jit(solution)/shard_map/ppermute | solution.py:48
  80.1 101.0 %copy-start.6 = (bf16[2,1024,512]{2,1,0:T(8,128)(2,1)S(1)}, bf16[2,1024,512]{2,1,0:T(8,128)(2,1)}, u32[]{:S(2)}) copy-start(bf16[2,1024,512]{2,1,0:T(8,128)(2,1)} %param.15) | copy-start | bytes 6291460
  80.1 49.9 %collective-permute-start.1 = (f32[2,256,1024]{2,1,0:T(8,128)S(1)}, f32[2,256,1024]{2,1,0:T(8,128)S(1)}, u32[]{:S(2)}, u32[]{:S(2)}) collective-permute-start(f32[2,256,1024]{2,1,0:T(8,128)S(1)} %add.141), channel_id=1, source_target_pairs={{0,128},{64,192},{128,0},{192,64},{256,384},{320,448},{384,256},{4... | collective-permute-start | bytes 6291464 | tf_op jit(solution)/shard_map/ppermute | solution.py:48
  130.6 50.5 %collective-permute-start.2 = (f32[2,256,1024]{2,1,0:T(8,128)S(1)}, f32[2,256,1024]{2,1,0:T(8,128)S(1)}, u32[]{:S(2)}, u32[]{:S(2)}) collective-permute-start(f32[2,256,1024]{2,1,0:T(8,128)S(1)} %add.142), channel_id=1, source_target_pairs={{0,256},{64,320},{128,384},{192,448},{256,0},{320,64},{384,128},{4... | collective-permute-start | bytes 6291464 | tf_op jit(solution)/shard_map/ppermute | solution.py:48
  181.8 7.9 %copy-start.3 = (f32[128,8]{0,1:T(8,128)S(1)}, f32[128,8]{0,1:T(8,128)}, u32[]{:S(2)}) copy-start(f32[128,8]{0,1:T(8,128)} %param.10) | copy-start | bytes 12292
  181.8 8.0 %copy-start.2 = (s32[128]{0:T(128)S(1)}, s32[128]{0:T(128)}, u32[]{:S(2)}) copy-start(s32[128]{0:T(128)} %param.13) | copy-start | bytes 1540
  181.8 8.5 %copy-start.5 = (s32[128]{0:T(128)S(1)}, s32[128]{0:T(128)}, u32[]{:S(2)}) copy-start(s32[128]{0:T(128)} %param.11) | copy-start | bytes 1540
  182.9 36.6 %all-to-all-start.1 = ((bf16[2,64,4,512]{3,2,0,1:T(4,128)(2,1)}), bf16[2,64,4,512]{3,2,0,1:T(4,128)(2,1)S(1)}, u32[]{:S(2)}, u32[]{:S(2)}) async-start(bf16[2,64,4,512]{3,2,0,1:T(4,128)(2,1)} %copy.24), calls=%async_computation.1 | async-start | bytes 1048576 | tf_op jit(solution)/shard_map/all_to_all | solution.py:56
